TPU v7x, 32 devices: a whole 2x2x4 slice. The times are simulated.
32 devices in a mesh: pipe: 4 (over x, core), tensor: 8 (over z, y).
Axes of the slice: x: 2, y: 2, z: 4, core: 2. Of those that a mesh axis runs over, the one named last changes fastest.
Arguments:
- stretch: bfloat16 [768, 7168], P(('pipe', 'tensor')), may hold values from -6 to 6
- ln_gain: float32 [7168], replicated, may hold values from 0.5 to 1.5
- ln_bias: float32 [7168], replicated, may hold values from -1.75 to 1.75
- qkv_weight: bfloat16 [7168, 12288], P(None, 'tensor'), may hold values from -0.0625 to 0.0625
- qkv_bias: float32 [12288], P('tensor'), may hold values from -1.75 to 1.75
- out_weight: bfloat16 [4096, 7168], P('tensor'), may hold values from -0.09375 to 0.09375
- out_bias: float32 [7168], replicated, may hold values from -1.75 to 1.75
- segment_ids: int32 [768], P('pipe'), may hold values from 0 to 31, never falling along the last dimension, each value on 1 to 96 neighbouring positions
- prefill_cache: bfloat16 [1, 32, 2, 128, 4096], P(None, ('pipe', 'tensor')), may hold values from -6 to 6
- block_dest: int32 [1, 32, 1], P(None, 'pipe'), may hold values from 0 to 3; in each aligned block of 8 rows (0 to 7, 8 to 15, ..., all dimensions but the last counted through in order) at most 3 rows name the same one
Outputs:
- mixed: bfloat16 [768, 7168], P(('pipe', 'tensor'))
- decode_side_cache: bfloat16 [1, 48, 2, 128, 4096], P(None, 'pipe', None, None, 'tensor')
Inputs may be any that keep to these rules, and one draw needn't show every extreme that they name: `block_dest`: among the 8 blocks of one group and one layer no decode group is named more than 3 times, and some decode group exactly 3 times. `segment_ids`: never falling along the tokens; a request spans at most 96 tokens.
All inputs are finite; a program needn't handle non-finite values.
Results may differ from a plain program's by a relative error of at most 0.013.
Values may be sent and summed in bfloat16 or wider, within the bound.
No kernel may reach another device: no remote copies, remote signals or barrier semaphores. Data moves between devices by JAX's collectives and lax.ppermute only.
A program may use at most 128 MiB of HBM per device.

v0:
```python
import jax
import jax.numpy as jnp
from jax import lax
from jax.sharding import PartitionSpec as P

HD = 128
RELAY_STEP = 0
CACHE_STEP = 2
CHAIN_PARTNER = True
CHAIN_RELAY = True


def normalize(x, gain, shift):
    mean = jnp.mean(x, axis=-1, keepdims=True)
    var = jnp.mean((x - mean) * (x - mean), axis=-1, keepdims=True)
    return ((x - mean) * lax.rsqrt(var + 1e-05) * gain + shift).astype(jnp.bfloat16)


def shifted(x, axis, k, n):
    return lax.ppermute(x, axis, [(j, (j + k) % n) for j in range(n)])


def split_heads(prefill_cache):
    tensor_count = lax.axis_size("tensor")
    layers, _, two, blk, width = prefill_cache.shape
    local_heads = width // tensor_count // HD
    split = prefill_cache.reshape(layers, two, blk, tensor_count, local_heads, HD)
    return jnp.transpose(split, (0, 1, 4, 3, 2, 5))


def send_decode(per_head_rows, block_dest):
    layers, two, local_heads, row_blocks, blk, _ = per_head_rows.shape
    pipe_count = lax.axis_size("pipe")
    capacity = 3 * row_blocks // (2 * pipe_count)
    dest = block_dest[:, :, 0]
    onehot = (dest[:, :, None] == jnp.arange(pipe_count, dtype=jnp.int32)[None, None, :]).astype(
        jnp.int32
    )
    earlier_tokens = jnp.cumsum(onehot, axis=1) - onehot
    slot = jnp.sum(earlier_tokens * onehot, axis=-1)
    position = dest * capacity + slot
    i = lax.axis_index("pipe")
    outgoing = []
    for k in range(pipe_count):
        targets = (i + k) % pipe_count * capacity + jnp.arange(capacity, dtype=jnp.int32)
        placement_index = (position[:, None, :] == targets[None, :, None]).astype(jnp.bfloat16)
        piece = jnp.einsum(
            "gud,gohdtc->guothc", placement_index, per_head_rows, preferred_element_type=jnp.float32
        ).astype(jnp.bfloat16)
        outgoing.append(piece.reshape((layers, capacity, two, blk, local_heads * HD)))
    return outgoing


def receive_decode(outgoing):
    pipe_count = lax.axis_size("pipe")
    i = lax.axis_index("pipe")
    layers, capacity = outgoing[0].shape[:2]
    arrived = jnp.zeros((layers, pipe_count * capacity) + outgoing[0].shape[2:], outgoing[0].dtype)
    previous = None
    for k in range(pipe_count):
        piece = outgoing[k]
        if k > 0:
            if previous is not None and CHAIN_RELAY:
                piece, previous = lax.optimization_barrier((piece, previous))
            piece = shifted(piece, "pipe", k, pipe_count)
            previous = piece
        arrived = lax.dynamic_update_slice_in_dim(
            arrived, piece, (i - k) % pipe_count * capacity, axis=1
        )
    return arrived


def partner(x):
    tensor_count = lax.axis_size("tensor")
    return lax.ppermute(x, "tensor", [(j, j ^ 1) for j in range(tensor_count)])


def ring(x):
    tensor_count = lax.axis_size("tensor")
    rows = tensor_count // 2
    return lax.ppermute(
        x, "tensor", [(j, (j // 2 + 1) % rows * 2 + j % 2) for j in range(tensor_count)]
    )


def gather_tokens(x, rider):
    tensor_count = lax.axis_size("tensor")
    rows = tensor_count // 2
    i = lax.axis_index("tensor")
    outer, inner = (i // 2, i % 2)
    own = [x]
    for k in range(1, rows):
        own.append(ring(own[-1]))
        if k == CACHE_STEP:
            own[-1], rider = lax.optimization_barrier((own[-1], rider))
    other = [partner(piece) for piece in own]
    steps = jnp.arange(rows)
    source = jnp.concatenate(
        [(outer - steps) % rows * 2 + inner, (outer - steps) % rows * 2 + (1 - inner)]
    )
    return (jnp.concatenate(own + other, axis=0), source, rider)


def scatter_tokens(partial, rider):
    tensor_count = lax.axis_size("tensor")
    rows = tensor_count // 2
    kept = partial[0].reshape((rows, -1) + partial[0].shape[1:])
    sent = partial[1].astype(jnp.bfloat16).reshape((rows, -1) + partial[1].shape[1:])
    mine = [None] * rows
    previous = None
    for s in [(s + 1) % rows for s in range(rows)]:
        piece = sent[s]
        if previous is not None and CHAIN_PARTNER:
            piece, previous = lax.optimization_barrier((piece, previous))
        previous = partner(piece)
        mine[s] = kept[s] + previous.astype(jnp.float32)
    carried = mine[1 % rows]
    for k in range(1, rows):
        if k == RELAY_STEP:
            carried, rider = lax.optimization_barrier((carried, rider))
        arrived = ring(carried.astype(jnp.bfloat16)).astype(jnp.float32)
        carried = arrived + mine[(k + 1) % rows]
    return (carried, rider)


def local(
    stretch,
    ln_gain,
    ln_bias,
    qkv_weight,
    qkv_bias,
    out_weight,
    out_bias,
    segment_ids,
    prefill_cache,
    block_dest,
):
    hidden = stretch.astype(jnp.float32)
    head_count = qkv_weight.shape[1] // (3 * HD)
    normed = normalize(hidden, ln_gain, ln_bias)
    split = split_heads(prefill_cache)
    gathered, source, split = gather_tokens(normed, split)
    if CACHE_STEP == 0:
        gathered, split = lax.optimization_barrier((gathered, split))
    per_head_rows = lax.all_to_all(split, "tensor", split_axis=3, concat_axis=3, tiled=True)
    outgoing = send_decode(per_head_rows, block_dest)
    qkv = (jnp.dot(gathered, qkv_weight, preferred_element_type=jnp.float32) + qkv_bias).astype(
        jnp.bfloat16
    )
    group_tokens = qkv.shape[0]
    place = (source[:, None] * normed.shape[0] + jnp.arange(normed.shape[0])[None, :]).reshape(-1)
    first_segment = segment_ids[0]
    segment_ids = segment_ids[place]
    heads = qkv.reshape(group_tokens, head_count, 3, HD)
    query = heads[:, :, 0]
    keys = heads[:, :, 1]
    value_rows = heads[:, :, 2]
    finished = per_head_rows[0]
    prefix_length = finished.shape[2] * finished.shape[3]
    cached_keys = finished[0].reshape(head_count, prefix_length, HD)
    old_values = finished[1].reshape(head_count, prefix_length, HD)
    scale = HD ** (-0.5)
    own_scores = jnp.einsum("qhd,khd->hqk", query, keys, preferred_element_type=jnp.float32) * scale
    old_scores = (
        jnp.einsum("qhd,hkd->hqk", query, cached_keys, preferred_element_type=jnp.float32) * scale
    )
    own_visible = (segment_ids[:, None] == segment_ids[None, :]) & (
        place[None, :] <= place[:, None]
    )
    old_visible = (segment_ids == first_segment)[:, None]
    own_scores = jnp.where(own_visible[None], own_scores, -jnp.inf)
    old_scores = jnp.where(old_visible[None], old_scores, -jnp.inf)
    scores = jnp.concatenate([old_scores, own_scores], axis=2)
    weights = jax.nn.softmax(scores, axis=-1).astype(jnp.bfloat16)
    context = jnp.einsum(
        "hqk,hkd->qhd",
        weights[:, :, :prefix_length],
        old_values,
        preferred_element_type=jnp.float32,
    )
    context = context + jnp.einsum(
        "hqk,khd->qhd",
        weights[:, :, prefix_length:],
        value_rows,
        preferred_element_type=jnp.float32,
    )
    context = context.astype(jnp.bfloat16).reshape(group_tokens, head_count * HD)
    decode_side_cache = receive_decode(outgoing)
    half = context.shape[0] // 2
    summed, decode_side_cache = scatter_tokens(
        [
            jnp.dot(context[:half], out_weight, preferred_element_type=jnp.float32),
            jnp.dot(context[half:], out_weight, preferred_element_type=jnp.bfloat16),
        ],
        decode_side_cache,
    )
    mixed = (hidden + summed + out_bias).astype(jnp.bfloat16)
    return (mixed, decode_side_cache)


def solution(mesh):
    return jax.shard_map(
        local,
        mesh=mesh,
        in_specs=(
            P(("pipe", "tensor"), None),
            P(),
            P(),
            P(None, "tensor"),
            P("tensor"),
            P("tensor", None),
            P(),
            P("pipe"),
            P(None, ("pipe", "tensor"), None, None, None),
            P(None, "pipe", None),
        ),
        out_specs=(P(("pipe", "tensor"), None), P(None, "pipe", None, None, "tensor")),
        check_vma=False,
    )
```

profile of v0, /device:TPU:1, one launch (start us, length us, event | category | flops | bytes accessed | tf_op | source)
XLA Modules:
  0.0 148.5 jit_solution(5265712922754977024)
XLA Ops:
  3.1 1.9 %constant_dynamic-update-slice_fusion.7 = (bf16[192,7168]{1,0:T(8,128)(2,1)}, bf16[24,7168]{1,0:T(8,128)(2,1)S(1)}) fusion(f32[7168]{0:T(1024)} %param.12, f32[7168]{0:T(1024)} %param.11, f32[24]{0:T(128)S(1)} %add_rsqrt_fusion, f32[24]{0:T(128)S(1)} %broadcast_multiply_fusion, bf16[24,7168]{1,0:T(8,128)(2,1)} %param.10), kind=kLoop, calls=%fused_computation.77 | loop fusion | flops 1032191 | bytes 1089728
  5.0 2.1 %collective-permute-start = (bf16[24,7168]{1,0:T(8,128)(2,1)S(1)}, bf16[24,7168]{1,0:T(8,128)(2,1)S(1)}, u32[]{:S(2)}, u32[]{:S(2)}) collective-permute-start(bf16[24,7168]{1,0:T(8,128)(2,1)S(1)} %get-tuple-element.17), channel_id=1, source_target_pairs={{0,2},{1,3},{2,4},{3,5},{4,6},{5,7},{6,0},{7,1},{8,10},{9,11},{10,... | collective-permute-start | bytes 1032200 | tf_op jit(solution)/shard_map/ppermute | solution.py:81
  9.8 2.0 %gather_fusion = s32[192]{0:T(256)S(1)} fusion(s32[192]{0:T(256)} %param.17, s32[1024]{0:T(1024)S(1)} %pad_clamp_fusion), kind=kCustom, calls=%fused_computation | custom fusion | bytes 2304 | tf_op jit(solution)/shard_map/gather | solution.py:153
  12.8 3.1 %copy.52 = bf16[1,1,2,128,4096]{3,4,2,1,0:T(8,128)(2,1)S(1)} copy(bf16[1,1,2,128,4096]{4,3,2,1,0:T(8,128)(2,1)} %param.18) | data formatting | bytes 4194304 | tf_op args[8]
  18.7 8.4 %collective-permute-done.1 = bf16[24,7168]{1,0:T(8,128)(2,1)S(1)} collective-permute-done((bf16[24,7168]{1,0:T(8,128)(2,1)S(1)}, bf16[24,7168]{1,0:T(8,128)(2,1)S(1)}, u32[]{:S(2)}, u32[]{:S(2)}) %collective-permute-start.1) | collective-permute-done | bytes 344096 | tf_op jit(solution)/shard_map/ppermute | solution.py:81
  28.6 2.6 %copy.53 = bf16[1,2,4,8,128,128]{5,4,2,1,0,3:T(8,128)(2,1)} copy(bf16[1,2,4,8,128,128]{4,5,2,3,1,0:T(8,128)(2,1)S(1)} %bitcast.110) | data formatting | bytes 4194304 | tf_op jit(solution)/shard_map/optimization_barrier | solution.py:95
  31.2 5.0 %all-to-all-start = ((bf16[1,2,4,8,128,128]{5,4,2,1,0,3:T(8,128)(2,1)}), bf16[1,2,4,8,128,128]{5,4,2,1,0,3:T(8,128)(2,1)S(1)}, u32[]{:S(2)}, u32[]{:S(2)}) async-start(bf16[1,2,4,8,128,128]{5,4,2,1,0,3:T(8,128)(2,1)} %copy.53), calls=%async_computation | async-start | bytes 4194304 | tf_op jit(solution)/shard_map/all_to_all | solution.py:145
  37.7 1.8 %constant_dynamic-update-slice_fusion.4 = bf16[192,7168]{1,0:T(8,128)(2,1)} fusion(bf16[192,7168]{1,0:T(8,128)(2,1)} %constant_dynamic-update-slice_fusion.5, bf16[24,7168]{1,0:T(8,128)(2,1)} %collective-permute-done.2), kind=kLoop, calls=%fused_computation.74 | loop fusion | bytes 688128
  42.0 1.7 %constant_dynamic-update-slice_fusion.1 = bf16[192,7168]{1,0:T(8,128)(2,1)} fusion(bf16[192,7168]{1,0:T(8,128)(2,1)} %constant_dynamic-update-slice_fusion.2, bf16[24,7168]{1,0:T(8,128)(2,1)} %collective-permute-done.5), kind=kLoop, calls=%fused_computation.71 | loop fusion | bytes 688128
  43.7 18.3 %collective-permute-done.6 = bf16[24,7168]{1,0:T(8,128)(2,1)S(1)} collective-permute-done((bf16[24,7168]{1,0:T(8,128)(2,1)}, bf16[24,7168]{1,0:T(8,128)(2,1)S(1)}, u32[]{:S(2)}, u32[]{:S(2)}) %collective-permute-start.6) | collective-permute-done | bytes 344096 | tf_op jit(solution)/shard_map/ppermute | solution.py:75
  62.7 13.3 %fusion.2 = bf16[192,1536]{1,0:T(8,128)(2,1)} fusion(bf16[192,7168]{1,0:T(8,128)(2,1)} %constant_dynamic-update-slice_fusion, bf16[7168,1536]{1,0:T(8,128)(2,1)} %param.13, f32[1536]{0:T(1024)S(1)} %copy-done.7), kind=kOutput, calls=%fused_computation.7 | convolution fusion | flops 4228448256 | bytes 25368576 | tf_op jit(solution)/shard_map/dot_general | solution.py:147
  79.4 2.2 %all-to-all-done = bf16[1,2,4,8,128,128]{5,4,2,1,0,3:T(8,128)(2,1)S(1)} async-done(((bf16[1,2,4,8,128,128]{5,4,2,1,0,3:T(8,128)(2,1)}), bf16[1,2,4,8,128,128]{5,4,2,1,0,3:T(8,128)(2,1)S(1)}, u32[]{:S(2)}, u32[]{:S(2)}) %all-to-all-start) | async-done | bytes 2097184 | tf_op jit(solution)/shard_map/all_to_all | solution.py:145
  89.0 3.4 %collective-permute-start.7 = (bf16[24,7168]{1,0:T(8,128)(2,1)S(1)}, bf16[24,7168]{1,0:T(8,128)(2,1)S(1)}, u32[]{:S(2)}, u32[]{:S(2)}) collective-permute-start(bf16[24,7168]{1,0:T(8,128)(2,1)S(1)} %get-tuple-element.20), channel_id=1, source_target_pairs={{0,1},{1,0},{2,3},{3,2},{4,5},{5,4},{6,7},{7,6},{8,9},{9,8},{10,11... | collective-permute-start | bytes 1032200 | tf_op jit(solution)/shard_map/ppermute | solution.py:75
  93.8 4.7 %collective-permute-done.7 = bf16[24,7168]{1,0:T(8,128)(2,1)S(1)} collective-permute-done((bf16[24,7168]{1,0:T(8,128)(2,1)S(1)}, bf16[24,7168]{1,0:T(8,128)(2,1)S(1)}, u32[]{:S(2)}, u32[]{:S(2)}) %collective-permute-start.7) | collective-permute-done | bytes 344096 | tf_op jit(solution)/shard_map/ppermute | solution.py:75
  98.5 2.0 %collective-permute-start.9 = (bf16[24,7168]{1,0:T(8,128)(2,1)}, bf16[24,7168]{1,0:T(8,128)(2,1)S(1)}, u32[]{:S(2)}, u32[]{:S(2)}) collective-permute-start(bf16[24,7168]{1,0:T(8,128)(2,1)} %get-tuple-element.11), channel_id=1, source_target_pairs={{0,1},{1,0},{2,3},{3,2},{4,5},{5,4},{6,7},{7,6},{8,9},{9,8},{10,11... | collective-permute-start | bytes 1032200 | tf_op jit(solution)/shard_map/ppermute | solution.py:75
  104.1 3.3 %collective-permute-start.14 = (bf16[1,3,2,128,512]{3,4,2,1,0:T(8,128)(2,1)}, bf16[1,3,2,128,512]{3,4,2,1,0:T(8,128)(2,1)}, u32[]{:S(2)}, u32[]{:S(2)}) collective-permute-start(bf16[1,3,2,128,512]{3,4,2,1,0:T(8,128)(2,1)} %bitcast.115), channel_id=1, source_target_pairs={{0,8},{8,16},{16,24},{24,0},{1,9},{9,17},{17,25},{25,1},{2,10},{10... | collective-permute-start | bytes 2359304 | tf_op jit(solution)/shard_map/ppermute | solution.py:20
  107.9 2.5 %collective-permute-done.8 = bf16[24,7168]{1,0:T(8,128)(2,1)} collective-permute-done((bf16[24,7168]{1,0:T(8,128)(2,1)}, bf16[24,7168]{1,0:T(8,128)(2,1)}, u32[]{:S(2)}, u32[]{:S(2)}) %collective-permute-start.8) | collective-permute-done | bytes 344096 | tf_op jit(solution)/shard_map/ppermute | solution.py:81
  110.3 2.0 %fusion.63 = bf16[24,7168]{1,0:T(8,128)(2,1)} fusion(f32[96,7168]{1,0:T(8,128)} %copy-done, bf16[24,7168]{1,0:T(8,128)(2,1)S(1)} %collective-permute-done.9, bf16[24,7168]{1,0:T(8,128)(2,1)} %collective-permute-done.8), kind=kLoop, calls=%fused_computation.53 | loop fusion | flops 860160 | bytes 1720320 | tf_op jit(solution)/shard_map/convert_element_type | solution.py:121
  117.5 3.1 %collective-permute-done.10 = bf16[24,7168]{1,0:T(8,128)(2,1)} collective-permute-done((bf16[24,7168]{1,0:T(8,128)(2,1)}, bf16[24,7168]{1,0:T(8,128)(2,1)}, u32[]{:S(2)}, u32[]{:S(2)}) %collective-permute-start.10) | collective-permute-done | bytes 344096 | tf_op jit(solution)/shard_map/ppermute | solution.py:81
  123.0 2.4 %fusion.25 = bf16[1,3,2,128,4,128]{5,1,3,4,2,0:T(4,128)(2,1)} fusion(bf16[1,2,4,8,128,128]{5,4,2,1,0,3:T(8,128)(2,1)S(1)} %all-to-all-done, s32[8]{0:T(128)S(1)} %multiply_add_fusion, s32[3]{0:T(128)S(1)} %iota_add_fusion.1), kind=kOutput, calls=%fused_computation.22 | convolution fusion | flops 6684696 | bytes 2883628 | tf_op jit(solution)/shard_map/gud,gohdtc->guothc/dot_general | solution.py:47
  127.3 2.0 %broadcast_in_dim.22 = bf16[1,12,2,128,512]{4,3,2,1,0:T(8,128)(2,1)} broadcast(bf16[]{:T(256)} %constant.111.clone.1), dimensions={} | broadcast | bytes 3145730 | tf_op jit(solution)/shard_map/broadcast_in_dim | solution.py:58
  132.6 4.4 %collective-permute-start.16 = (bf16[1,3,2,128,512]{3,4,2,1,0:T(8,128)(2,1)S(1)}, bf16[1,3,2,128,512]{3,4,2,1,0:T(8,128)(2,1)S(1)}, u32[]{:S(2)}, u32[]{:S(2)}) collective-permute-start(bf16[1,3,2,128,512]{3,4,2,1,0:T(8,128)(2,1)S(1)} %bitcast.114), channel_id=1, source_target_pairs={{0,24},{8,0},{16,8},{24,16},{1,25},{9,1},{17,9},{25,17},{2,26},{10... | collective-permute-start | bytes 2359304 | tf_op jit(solution)/shard_map/ppermute | solution.py:20
  137.0 2.2 %fusion.58 = bf16[24,7168]{1,0:T(8,128)(2,1)} fusion(bf16[24,7168]{1,0:T(8,128)(2,1)S(1)} %copy-done.1, f32[96,7168]{1,0:T(8,128)} %copy-done, bf16[24,7168]{1,0:T(8,128)(2,1)} %collective-permute-done.13, bf16[24,7168]{1,0:T(8,128)(2,1)} %collective-permute-done.12, f32[7168]{0:T(1024)S(1)} %copy-done.5), kind=kLoop, calls=%fused_computation.45 | loop fusion | flops 1376256 | bytes 2093056 | tf_op jit(solution)/shard_map/convert_element_type | solution.py:197
  141.5 5.8 %collective-permute-done.16 = bf16[1,3,2,128,512]{3,4,2,1,0:T(8,128)(2,1)S(1)} collective-permute-done((bf16[1,3,2,128,512]{3,4,2,1,0:T(8,128)(2,1)S(1)}, bf16[1,3,2,128,512]{3,4,2,1,0:T(8,128)(2,1)S(1)}, u32[]{:S(2)}, u32[]{:S(2)}) %collective-permute-start.16) | collective-permute-done | bytes 786464 | tf_op jit(solution)/shard_map/ppermute | solution.py:20
  (104 shorter events, 47.4 us)
Async XLA Ops:
  0.6 11.2 %copy-start.6 = (s32[1,8,1]{1,2,0:T(1,128)S(1)}, s32[1,8,1]{1,2,0:T(1,128)}, u32[]{:S(2)}) copy-start(s32[1,8,1]{1,2,0:T(1,128)} %param.19) | copy-start | bytes 100
  5.0 11.9 %collective-permute-start = (bf16[24,7168]{1,0:T(8,128)(2,1)S(1)}, bf16[24,7168]{1,0:T(8,128)(2,1)S(1)}, u32[]{:S(2)}, u32[]{:S(2)}) collective-permute-start(bf16[24,7168]{1,0:T(8,128)(2,1)S(1)} %get-tuple-element.17), channel_id=1, source_target_pairs={{0,2},{1,3},{2,4},{3,5},{4,6},{5,7},{6,0},{7,1},{8,10},{9,11},{10,... | collective-permute-start | bytes 1032200 | tf_op jit(solution)/shard_map/ppermute | solution.py:81
  7.1 32.3 %collective-permute-start.3 = (bf16[24,7168]{1,0:T(8,128)(2,1)S(1)}, bf16[24,7168]{1,0:T(8,128)(2,1)S(1)}, u32[]{:S(2)}, u32[]{:S(2)}) collective-permute-start(bf16[24,7168]{1,0:T(8,128)(2,1)S(1)} %get-tuple-element.17), channel_id=1, source_target_pairs={{0,1},{1,0},{2,3},{3,2},{4,5},{5,4},{6,7},{7,6},{8,9},{9,8},{10,11... | collective-permute-start | bytes 1032200 | tf_op jit(solution)/shard_map/ppermute | solution.py:75
  16.9 10.1 %collective-permute-start.1 = (bf16[24,7168]{1,0:T(8,128)(2,1)S(1)}, bf16[24,7168]{1,0:T(8,128)(2,1)S(1)}, u32[]{:S(2)}, u32[]{:S(2)}) collective-permute-start(bf16[24,7168]{1,0:T(8,128)(2,1)S(1)} %collective-permute-done), channel_id=1, source_target_pairs={{0,2},{1,3},{2,4},{3,5},{4,6},{5,7},{6,0},{7,1},{8,10},{9,11},{10,... | collective-permute-start | bytes 1032200 | tf_op jit(solution)/shard_map/ppermute | solution.py:81
  17.5 22.8 %collective-permute-start.4 = (bf16[24,7168]{1,0:T(8,128)(2,1)S(1)}, bf16[24,7168]{1,0:T(8,128)(2,1)}, u32[]{:S(2)}, u32[]{:S(2)}) collective-permute-start(bf16[24,7168]{1,0:T(8,128)(2,1)S(1)} %collective-permute-done), channel_id=1, source_target_pairs={{0,1},{1,0},{2,3},{3,2},{4,5},{5,4},{6,7},{7,6},{8,9},{9,8},{10,11... | collective-permute-start | bytes 1032200 | tf_op jit(solution)/shard_map/ppermute | solution.py:75
  27.1 9.3 %collective-permute-start.2 = (bf16[24,7168]{1,0:T(8,128)(2,1)S(1)}, bf16[24,7168]{1,0:T(8,128)(2,1)}, u32[]{:S(2)}, u32[]{:S(2)}) collective-permute-start(bf16[24,7168]{1,0:T(8,128)(2,1)S(1)} %collective-permute-done.1), channel_id=1, source_target_pairs={{0,2},{1,3},{2,4},{3,5},{4,6},{5,7},{6,0},{7,1},{8,10},{9,11},{10,... | collective-permute-start | bytes 1032200 | tf_op jit(solution)/shard_map/ppermute | solution.py:81
  27.1 14.9 %collective-permute-start.5 = (bf16[24,7168]{1,0:T(8,128)(2,1)S(1)}, bf16[24,7168]{1,0:T(8,128)(2,1)}, u32[]{:S(2)}, u32[]{:S(2)}) collective-permute-start(bf16[24,7168]{1,0:T(8,128)(2,1)S(1)} %collective-permute-done.1), channel_id=1, source_target_pairs={{0,1},{1,0},{2,3},{3,2},{4,5},{5,4},{6,7},{7,6},{8,9},{9,8},{10,11... | collective-permute-start | bytes 1032200 | tf_op jit(solution)/shard_map/ppermute | solution.py:75
  31.2 50.5 %all-to-all-start = ((bf16[1,2,4,8,128,128]{5,4,2,1,0,3:T(8,128)(2,1)}), bf16[1,2,4,8,128,128]{5,4,2,1,0,3:T(8,128)(2,1)S(1)}, u32[]{:S(2)}, u32[]{:S(2)}) async-start(bf16[1,2,4,8,128,128]{5,4,2,1,0,3:T(8,128)(2,1)} %copy.53), calls=%async_computation | async-start | bytes 4194304 | tf_op jit(solution)/shard_map/all_to_all | solution.py:145
  36.2 26.5 %copy-start.7 = (f32[1536]{0:T(1024)S(1)}, f32[1536]{0:T(1024)}, u32[]{:S(2)}) copy-start(f32[1536]{0:T(1024)} %param.14) | copy-start | bytes 18436
  36.4 25.6 %collective-permute-start.6 = (bf16[24,7168]{1,0:T(8,128)(2,1)}, bf16[24,7168]{1,0:T(8,128)(2,1)S(1)}, u32[]{:S(2)}, u32[]{:S(2)}) collective-permute-start(bf16[24,7168]{1,0:T(8,128)(2,1)} %collective-permute-done.2), channel_id=1, source_target_pairs={{0,1},{1,0},{2,3},{3,2},{4,5},{5,4},{6,7},{7,6},{8,9},{9,8},{10,11... | collective-permute-start | bytes 1032200 | tf_op jit(solution)/shard_map/ppermute | solution.py:75
  84.0 2.6 %slice-start.1 = ((s8[7340032]{0:T(1024)(128)(4,1)}), s8[4194304]{0:T(1024)(128)(4,1)S(1)}, s32[]{:S(2)}) async-start(s8[7340032]{0:T(1024)(128)(4,1)} %bitcast.108), calls=%async_computation.2 | async-start | bytes 8388608
  89.0 9.5 %collective-permute-start.7 = (bf16[24,7168]{1,0:T(8,128)(2,1)S(1)}, bf16[24,7168]{1,0:T(8,128)(2,1)S(1)}, u32[]{:S(2)}, u32[]{:S(2)}) collective-permute-start(bf16[24,7168]{1,0:T(8,128)(2,1)S(1)} %get-tuple-element.20), channel_id=1, source_target_pairs={{0,1},{1,0},{2,3},{3,2},{4,5},{5,4},{6,7},{7,6},{8,9},{9,8},{10,11... | collective-permute-start | bytes 1032200 | tf_op jit(solution)/shard_map/ppermute | solution.py:75
  93.8 6.7 %copy-start = (f32[96,7168]{1,0:T(8,128)}, f32[96,7168]{1,0:T(8,128)S(1)}, u32[]{:S(2)}) copy-start(f32[96,7168]{1,0:T(8,128)S(1)} %fusion.70) | copy-start | bytes 8257540
  98.5 9.0 %collective-permute-start.9 = (bf16[24,7168]{1,0:T(8,128)(2,1)}, bf16[24,7168]{1,0:T(8,128)(2,1)S(1)}, u32[]{:S(2)}, u32[]{:S(2)}) collective-permute-start(bf16[24,7168]{1,0:T(8,128)(2,1)} %get-tuple-element.11), channel_id=1, source_target_pairs={{0,1},{1,0},{2,3},{3,2},{4,5},{5,4},{6,7},{7,6},{8,9},{9,8},{10,11... | collective-permute-start | bytes 1032200 | tf_op jit(solution)/shard_map/ppermute | solution.py:75
  101.3 9.0 %collective-permute-start.8 = (bf16[24,7168]{1,0:T(8,128)(2,1)}, bf16[24,7168]{1,0:T(8,128)(2,1)}, u32[]{:S(2)}, u32[]{:S(2)}) collective-permute-start(bf16[24,7168]{1,0:T(8,128)(2,1)} %fusion.64), channel_id=1, source_target_pairs={{0,2},{1,3},{2,4},{3,5},{4,6},{5,7},{6,0},{7,1},{8,10},{9,11},{10,... | collective-permute-start | bytes 1032200 | tf_op jit(solution)/shard_map/ppermute | solution.py:81
  104.1 12.6 %collective-permute-start.14 = (bf16[1,3,2,128,512]{3,4,2,1,0:T(8,128)(2,1)}, bf16[1,3,2,128,512]{3,4,2,1,0:T(8,128)(2,1)}, u32[]{:S(2)}, u32[]{:S(2)}) collective-permute-start(bf16[1,3,2,128,512]{3,4,2,1,0:T(8,128)(2,1)} %bitcast.115), channel_id=1, source_target_pairs={{0,8},{8,16},{16,24},{24,0},{1,9},{9,17},{17,25},{25,1},{2,10},{10... | collective-permute-start | bytes 2359304 | tf_op jit(solution)/shard_map/ppermute | solution.py:20
  107.5 10.0 %collective-permute-start.11 = (bf16[24,7168]{1,0:T(8,128)(2,1)}, bf16[24,7168]{1,0:T(8,128)(2,1)}, u32[]{:S(2)}, u32[]{:S(2)}) collective-permute-start(bf16[24,7168]{1,0:T(8,128)(2,1)} %get-tuple-element.12), channel_id=1, source_target_pairs={{0,1},{1,0},{2,3},{3,2},{4,5},{5,4},{6,7},{7,6},{8,9},{9,8},{10,11... | collective-permute-start | bytes 1032200 | tf_op jit(solution)/shard_map/ppermute | solution.py:75
  112.4 8.2 %collective-permute-start.10 = (bf16[24,7168]{1,0:T(8,128)(2,1)}, bf16[24,7168]{1,0:T(8,128)(2,1)}, u32[]{:S(2)}, u32[]{:S(2)}) collective-permute-start(bf16[24,7168]{1,0:T(8,128)(2,1)} %fusion.63), channel_id=1, source_target_pairs={{0,2},{1,3},{2,4},{3,5},{4,6},{5,7},{6,0},{7,1},{8,10},{9,11},{10,... | collective-permute-start | bytes 1032200 | tf_op jit(solution)/shard_map/ppermute | solution.py:81
  116.7 15.9 %collective-permute-start.15 = (bf16[1,3,2,128,512]{3,4,2,1,0:T(8,128)(2,1)}, bf16[1,3,2,128,512]{3,4,2,1,0:T(8,128)(2,1)}, u32[]{:S(2)}, u32[]{:S(2)}) collective-permute-start(bf16[1,3,2,128,512]{3,4,2,1,0:T(8,128)(2,1)} %bitcast.26), channel_id=1, source_target_pairs={{0,16},{8,24},{16,0},{24,8},{1,17},{9,25},{17,1},{25,9},{2,18},{10... | collective-permute-start | bytes 2359304 | tf_op jit(solution)/shard_map/ppermute | solution.py:20
  117.5 19.5 %collective-permute-start.13 = (bf16[24,7168]{1,0:T(8,128)(2,1)}, bf16[24,7168]{1,0:T(8,128)(2,1)}, u32[]{:S(2)}, u32[]{:S(2)}) collective-permute-start(bf16[24,7168]{1,0:T(8,128)(2,1)} %get-tuple-element.13), channel_id=1, source_target_pairs={{0,1},{1,0},{2,3},{3,2},{4,5},{5,4},{6,7},{7,6},{8,9},{9,8},{10,11... | collective-permute-start | bytes 1032200 | tf_op jit(solution)/shard_map/ppermute | solution.py:75
  122.0 15.0 %collective-permute-start.12 = (bf16[24,7168]{1,0:T(8,128)(2,1)S(1)}, bf16[24,7168]{1,0:T(8,128)(2,1)}, u32[]{:S(2)}, u32[]{:S(2)}) collective-permute-start(bf16[24,7168]{1,0:T(8,128)(2,1)S(1)} %fusion.61), channel_id=1, source_target_pairs={{0,2},{1,3},{2,4},{3,5},{4,6},{5,7},{6,0},{7,1},{8,10},{9,11},{10,... | collective-permute-start | bytes 1032200 | tf_op jit(solution)/shard_map/ppermute | solution.py:81
  129.3 7.7 %copy-start.1 = (bf16[24,7168]{1,0:T(8,128)(2,1)S(1)}, bf16[24,7168]{1,0:T(8,128)(2,1)}, u32[]{:S(2)}) copy-start(bf16[24,7168]{1,0:T(8,128)(2,1)} %param.10) | copy-start | bytes 1032196
  129.3 7.7 %copy-start.5 = (f32[7168]{0:T(1024)S(1)}, f32[7168]{0:T(1024)}, u32[]{:S(2)}) copy-start(f32[7168]{0:T(1024)} %param.16) | copy-start | bytes 86020
  132.6 14.7 %collective-permute-start.16 = (bf16[1,3,2,128,512]{3,4,2,1,0:T(8,128)(2,1)S(1)}, bf16[1,3,2,128,512]{3,4,2,1,0:T(8,128)(2,1)S(1)}, u32[]{:S(2)}, u32[]{:S(2)}) collective-permute-start(bf16[1,3,2,128,512]{3,4,2,1,0:T(8,128)(2,1)S(1)} %bitcast.114), channel_id=1, source_target_pairs={{0,24},{8,0},{16,8},{24,16},{1,25},{9,1},{17,9},{25,17},{2,26},{10... | collective-permute-start | bytes 2359304 | tf_op jit(solution)/shard_map/ppermute | solution.py:20
  (4 other events, 5.5 us)
where the time goes:
time: 149 us
  waiting for transfers between devices  46 us (31%)
  local copies, waits for them, and re-layouts  36.6 us (25%)
  starting transfers between devices  26.7 us (18%)
  matrix products  24.8 us (17%)
  other arithmetic  13.5 us (9%)
    ppermute x8, waiting for transfers between devices, partner(): return lax.ppermute(x, 'tensor', [(j, j ^ 1) for j in range(tensor_count)])  23 us
    ppermute x6, waiting for transfers between devices, ring(): lax.ppermute(x, 'tensor', [(j, (j // 2 + 1) % rows * 2 + j % 2) for j in...  15 us
    dot_general x1, matrix products, local(): jnp.dot(gathered, qkv_weight, preferred_element_type=jnp.float32) + qkv_bias  13.3 us
    unnamed x28, local copies, waits for them, and re-layouts  13.1 us
    ppermute x8, starting transfers between devices, partner(): return lax.ppermute(x, 'tensor', [(j, j ^ 1) for j in range(tensor_count)])  9.62 us
    ppermute x3, starting transfers between devices, shifted(): return lax.ppermute(x, axis, [(j, (j + k) % n) for j in range(n)])  8.44 us
    dot_general x4, matrix products, send_decode(): jnp.einsum('gud,gohdtc->guothc', placement_index, per_head_rows, preferre...  6.77 us
    ppermute x3, waiting for transfers between devices, shifted(): return lax.ppermute(x, axis, [(j, (j + k) % n) for j in range(n)])  5.83 us
  transfers between devices with their start and end apart: 18, of which 10 were waited for; matrix products, arithmetic and copies ran while one was open for 41% of the time, Pallas kernels for 0%

commit v1 on v0

--- a/solution.py
+++ b/solution.py
@@ -142,7 +142,12 @@
     gathered, source, split = gather_tokens(normed, split)
     if CACHE_STEP == 0:
         gathered, split = lax.optimization_barrier((gathered, split))
-    per_head_rows = lax.all_to_all(split, "tensor", split_axis=3, concat_axis=3, tiled=True)
+    per_head_rows = jnp.concatenate(
+        lax.all_to_all(
+            jnp.stack(jnp.split(split, lax.axis_size("tensor"), axis=3)), "tensor", 0, 0
+        ),
+        axis=3,
+    )
     outgoing = send_decode(per_head_rows, block_dest)
     qkv = (jnp.dot(gathered, qkv_weight, preferred_element_type=jnp.float32) + qkv_bias).astype(
         jnp.bfloat16

time: 149 us -> 161 us (1.081)
  local copies, waits for them, and re-layouts: 36.6 us -> 48.4 us
    unnamed x28 -> x35, local copies, waits for them, and re-layouts: 13.1 us -> 20.9 us
    split x0 -> x9, local copies, waits for them, and re-layouts: none -> 5.24 us  [local(): jnp.split(split, lax.axis_size('tensor'), axis=3)]
    optimization_barrier x1 -> x0, local copies, waits for them, and re-layouts: 2.62 us -> none  [gather_tokens(): own[-1], rider = lax.optimization_barrier((own[-1], rider))]
    all_to_all x1, waiting for transfers between devices: 2.2 us -> 3.95 us  [local(): lax.all_to_all(jnp.stack(jnp.split(split, lax.axis_size('tensor'), axis=3...]
  transfers between devices with their start and end apart: 18 -> 18, of which waited for: 10 -> 10; matrix products, arithmetic and copies ran while one was open for 41% -> 44% of each run, Pallas kernels for 0% -> 0%
where the time goes in v1:
time: 161 us; the launch traced here: 160 us
  local copies, waits for them, and re-layouts  48.4 us (30%)
  waiting for transfers between devices  46.6 us (29%)
  starting transfers between devices  25.9 us (16%)
  matrix products  24 us (15%)
  other arithmetic  14.2 us (9%)
    ppermute x8, waiting for transfers between devices, partner(): return lax.ppermute(x, 'tensor', [(j, j ^ 1) for j in range(tensor_count)])  22 us
    unnamed x35, local copies, waits for them, and re-layouts  20.9 us
    ppermute x6, waiting for transfers between devices, ring(): lax.ppermute(x, 'tensor', [(j, (j // 2 + 1) % rows * 2 + j % 2) for j in...  14.4 us
    dot_general x1, matrix products, local(): jnp.dot(gathered, qkv_weight, preferred_element_type=jnp.float32) + qkv_bias  12.5 us
    ppermute x8, starting transfers between devices, partner(): return lax.ppermute(x, 'tensor', [(j, j ^ 1) for j in range(tensor_count)])  10.2 us
    ppermute x3, starting transfers between devices, shifted(): return lax.ppermute(x, axis, [(j, (j + k) % n) for j in range(n)])  8.01 us
    dot_general x4, matrix products, send_decode(): jnp.einsum('gud,gohdtc->guothc', placement_index, per_head_rows, preferre...  6.76 us
    ppermute x3, waiting for transfers between devices, shifted(): return lax.ppermute(x, axis, [(j, (j + k) % n) for j in range(n)])  6.26 us
  transfers between devices with their start and end apart: 18, of which 10 were waited for; matrix products, arithmetic and copies ran while one was open for 44% of the time, Pallas kernels for 0%

profile of v1, /device:TPU:1, one launch (start us, length us, event | category | flops | bytes accessed | tf_op | source)
XLA Modules:
  0.0 160.1 jit_solution(18251045343209871782)
XLA Ops:
  3.1 2.1 %constant_dynamic-update-slice_fusion.7 = (bf16[192,7168]{1,0:T(8,128)(2,1)}, bf16[24,7168]{1,0:T(8,128)(2,1)}) fusion(f32[7168]{0:T(1024)} %param.12, f32[7168]{0:T(1024)} %param.11, f32[24]{0:T(128)S(1)} %add_rsqrt_fusion, f32[24]{0:T(128)S(1)} %broadcast_multiply_fusion, bf16[24,7168]{1,0:T(8,128)(2,1)} %param.10), kind=kLoop, calls=%fused_computation.86 | loop fusion | flops 1032191 | bytes 1089728
  5.1 2.1 %collective-permute-start = (bf16[24,7168]{1,0:T(8,128)(2,1)}, bf16[24,7168]{1,0:T(8,128)(2,1)}, u32[]{:S(2)}, u32[]{:S(2)}) collective-permute-start(bf16[24,7168]{1,0:T(8,128)(2,1)} %get-tuple-element.17), channel_id=1, source_target_pairs={{0,2},{1,3},{2,4},{3,5},{4,6},{5,7},{6,0},{7,1},{8,10},{9,11},{10,... | collective-permute-start | bytes 1032200 | tf_op jit(solution)/shard_map/ppermute | solution.py:81
  9.9 2.0 %gather_fusion = s32[192]{0:T(256)S(1)} fusion(s32[192]{0:T(256)} %param.17, s32[1024]{0:T(1024)S(1)} %pad_clamp_fusion), kind=kCustom, calls=%fused_computation | custom fusion | bytes 2304 | tf_op jit(solution)/shard_map/gather | solution.py:158
  12.8 3.1 %copy.249 = bf16[1,1,2,128,4096]{3,4,2,1,0:T(8,128)(2,1)S(1)} copy(bf16[1,1,2,128,4096]{4,3,2,1,0:T(8,128)(2,1)} %param.18) | data formatting | bytes 4194304 | tf_op args[8]
  20.1 7.7 %collective-permute-done.1 = bf16[24,7168]{1,0:T(8,128)(2,1)} collective-permute-done((bf16[24,7168]{1,0:T(8,128)(2,1)}, bf16[24,7168]{1,0:T(8,128)(2,1)}, u32[]{:S(2)}, u32[]{:S(2)}) %collective-permute-start.1) | collective-permute-done | bytes 344096 | tf_op jit(solution)/shard_map/ppermute | solution.py:81
  28.6 1.8 %constant_dynamic-update-slice_fusion.5 = bf16[192,7168]{1,0:T(8,128)(2,1)} fusion(bf16[192,7168]{1,0:T(8,128)(2,1)} %constant_dynamic-update-slice_fusion.6, bf16[24,7168]{1,0:T(8,128)(2,1)} %collective-permute-done.1), kind=kLoop, calls=%fused_computation.84 | loop fusion | bytes 688128
  41.4 5.0 %all-to-all-start = ((bf16[8,1,2,4,1,128,128]{6,5,3,2,4,1,0:T(8,128)(2,1)}), bf16[8,1,2,4,1,128,128]{6,5,3,2,4,1,0:T(8,128)(2,1)S(1)}, u32[]{:S(2)}, u32[]{:S(2)}) async-start(bf16[8,1,2,4,1,128,128]{6,5,3,2,4,1,0:T(8,128)(2,1)} %bitcast_dynamic-update-slice_fusion), calls=%async_computation | async-start | bytes 4194304 | tf_op jit(solution)/shard_map/all_to_all | solution.py:146
  47.9 1.8 %constant_dynamic-update-slice_fusion.4 = bf16[192,7168]{1,0:T(8,128)(2,1)} fusion(bf16[192,7168]{1,0:T(8,128)(2,1)} %constant_dynamic-update-slice_fusion.5, bf16[24,7168]{1,0:T(8,128)(2,1)} %collective-permute-done.2), kind=kLoop, calls=%fused_computation.83 | loop fusion | bytes 688128
  54.9 17.3 %collective-permute-done.6 = bf16[24,7168]{1,0:T(8,128)(2,1)S(1)} collective-permute-done((bf16[24,7168]{1,0:T(8,128)(2,1)}, bf16[24,7168]{1,0:T(8,128)(2,1)S(1)}, u32[]{:S(2)}, u32[]{:S(2)}) %collective-permute-start.6) | collective-permute-done | bytes 344096 | tf_op jit(solution)/shard_map/ppermute | solution.py:75
  72.9 12.5 %fusion.2 = bf16[192,1536]{1,0:T(8,128)(2,1)S(1)} fusion(bf16[192,7168]{1,0:T(8,128)(2,1)} %constant_dynamic-update-slice_fusion, bf16[7168,1536]{1,0:T(8,128)(2,1)} %param.13, f32[1536]{0:T(1024)S(1)} %copy-done.7), kind=kOutput, calls=%fused_computation.7 | convolution fusion | flops 4228448256 | bytes 25368576 | tf_op jit(solution)/shard_map/dot_general | solution.py:152
  87.9 3.9 %all-to-all-done = bf16[8,1,2,4,1,128,128]{6,5,3,2,4,1,0:T(8,128)(2,1)S(1)} async-done(((bf16[8,1,2,4,1,128,128]{6,5,3,2,4,1,0:T(8,128)(2,1)}), bf16[8,1,2,4,1,128,128]{6,5,3,2,4,1,0:T(8,128)(2,1)S(1)}, u32[]{:S(2)}, u32[]{:S(2)}) %all-to-all-start) | async-done | bytes 2097184 | tf_op jit(solution)/shard_map/all_to_all | solution.py:146
  100.6 3.4 %collective-permute-start.7 = (bf16[24,7168]{1,0:T(8,128)(2,1)S(1)}, bf16[24,7168]{1,0:T(8,128)(2,1)S(1)}, u32[]{:S(2)}, u32[]{:S(2)}) collective-permute-start(bf16[24,7168]{1,0:T(8,128)(2,1)S(1)} %get-tuple-element.28), channel_id=1, source_target_pairs={{0,1},{1,0},{2,3},{3,2},{4,5},{5,4},{6,7},{7,6},{8,9},{9,8},{10,11... | collective-permute-start | bytes 1032200 | tf_op jit(solution)/shard_map/ppermute | solution.py:75
  105.4 4.7 %collective-permute-done.7 = bf16[24,7168]{1,0:T(8,128)(2,1)S(1)} collective-permute-done((bf16[24,7168]{1,0:T(8,128)(2,1)S(1)}, bf16[24,7168]{1,0:T(8,128)(2,1)S(1)}, u32[]{:S(2)}, u32[]{:S(2)}) %collective-permute-start.7) | collective-permute-done | bytes 344096 | tf_op jit(solution)/shard_map/ppermute | solution.py:75
  110.1 2.0 %collective-permute-start.9 = (bf16[24,7168]{1,0:T(8,128)(2,1)}, bf16[24,7168]{1,0:T(8,128)(2,1)S(1)}, u32[]{:S(2)}, u32[]{:S(2)}) collective-permute-start(bf16[24,7168]{1,0:T(8,128)(2,1)} %get-tuple-element.11), channel_id=1, source_target_pairs={{0,1},{1,0},{2,3},{3,2},{4,5},{5,4},{6,7},{7,6},{8,9},{9,8},{10,11... | collective-permute-start | bytes 1032200 | tf_op jit(solution)/shard_map/ppermute | solution.py:75
  116.2 2.8 %collective-permute-start.14 = (bf16[1,3,2,128,512]{3,4,2,1,0:T(8,128)(2,1)}, bf16[1,3,2,128,512]{3,4,2,1,0:T(8,128)(2,1)}, u32[]{:S(2)}, u32[]{:S(2)}) collective-permute-start(bf16[1,3,2,128,512]{3,4,2,1,0:T(8,128)(2,1)} %bitcast.136), channel_id=1, source_target_pairs={{0,8},{8,16},{16,24},{24,0},{1,9},{9,17},{17,25},{25,1},{2,10},{10... | collective-permute-start | bytes 2359304 | tf_op jit(solution)/shard_map/ppermute | solution.py:20
  119.5 2.4 %collective-permute-done.8 = bf16[24,7168]{1,0:T(8,128)(2,1)} collective-permute-done((bf16[24,7168]{1,0:T(8,128)(2,1)}, bf16[24,7168]{1,0:T(8,128)(2,1)}, u32[]{:S(2)}, u32[]{:S(2)}) %collective-permute-start.8) | collective-permute-done | bytes 344096 | tf_op jit(solution)/shard_map/ppermute | solution.py:81
  121.9 2.0 %fusion.63 = bf16[24,7168]{1,0:T(8,128)(2,1)} fusion(f32[96,7168]{1,0:T(8,128)} %copy-done, bf16[24,7168]{1,0:T(8,128)(2,1)S(1)} %collective-permute-done.9, bf16[24,7168]{1,0:T(8,128)(2,1)} %collective-permute-done.8), kind=kLoop, calls=%fused_computation.54 | loop fusion | flops 860160 | bytes 1720320 | tf_op jit(solution)/shard_map/convert_element_type | solution.py:121
  129.0 3.0 %collective-permute-done.10 = bf16[24,7168]{1,0:T(8,128)(2,1)S(1)} collective-permute-done((bf16[24,7168]{1,0:T(8,128)(2,1)}, bf16[24,7168]{1,0:T(8,128)(2,1)S(1)}, u32[]{:S(2)}, u32[]{:S(2)}) %collective-permute-start.10) | collective-permute-done | bytes 344096 | tf_op jit(solution)/shard_map/ppermute | solution.py:81
  132.0 2.0 %fusion.61 = bf16[24,7168]{1,0:T(8,128)(2,1)} fusion(f32[96,7168]{1,0:T(8,128)} %copy-done, bf16[24,7168]{1,0:T(8,128)(2,1)} %collective-permute-done.11, bf16[24,7168]{1,0:T(8,128)(2,1)S(1)} %collective-permute-done.10), kind=kLoop, calls=%fused_computation.51 | loop fusion | flops 860160 | bytes 1720320 | tf_op jit(solution)/shard_map/convert_element_type | solution.py:121
  134.0 2.4 %fusion.25 = bf16[1,3,2,128,4,128]{5,1,3,4,2,0:T(4,128)(2,1)} fusion(bf16[8,1,2,4,1,128,128]{6,5,3,2,4,1,0:T(8,128)(2,1)S(1)} %all-to-all-done, s32[8]{0:T(128)S(1)} %multiply_add_fusion, s32[3]{0:T(128)S(1)} %iota_add_fusion.1), kind=kOutput, calls=%fused_computation.22 | convolution fusion | flops 6684696 | bytes 2883628 | tf_op jit(solution)/shard_map/gud,gohdtc->guothc/dot_general | solution.py:47
  138.4 2.0 %broadcast_in_dim.22 = bf16[1,12,2,128,512]{4,3,2,1,0:T(8,128)(2,1)} broadcast(bf16[]{:T(256)} %constant.111.clone.1), dimensions={} | broadcast | bytes 3145730 | tf_op jit(solution)/shard_map/broadcast_in_dim | solution.py:58
  144.1 4.4 %collective-permute-start.16 = (bf16[1,3,2,128,512]{3,4,2,1,0:T(8,128)(2,1)S(1)}, bf16[1,3,2,128,512]{3,4,2,1,0:T(8,128)(2,1)S(1)}, u32[]{:S(2)}, u32[]{:S(2)}) collective-permute-start(bf16[1,3,2,128,512]{3,4,2,1,0:T(8,128)(2,1)S(1)} %bitcast.135), channel_id=1, source_target_pairs={{0,24},{8,0},{16,8},{24,16},{1,25},{9,1},{17,9},{25,17},{2,26},{10... | collective-permute-start | bytes 2359304 | tf_op jit(solution)/shard_map/ppermute | solution.py:20
  148.6 2.2 %fusion.58 = bf16[24,7168]{1,0:T(8,128)(2,1)} fusion(bf16[24,7168]{1,0:T(8,128)(2,1)S(1)} %copy-done.1, f32[96,7168]{1,0:T(8,128)} %copy-done, bf16[24,7168]{1,0:T(8,128)(2,1)} %collective-permute-done.13, bf16[24,7168]{1,0:T(8,128)(2,1)} %collective-permute-done.12, f32[7168]{0:T(1024)S(1)} %copy-done.5), kind=kLoop, calls=%fused_computation.46 | loop fusion | flops 1376256 | bytes 2093056 | tf_op jit(solution)/shard_map/convert_element_type | solution.py:202
  153.1 5.7 %collective-permute-done.16 = bf16[1,3,2,128,512]{3,4,2,1,0:T(8,128)(2,1)S(1)} collective-permute-done((bf16[1,3,2,128,512]{3,4,2,1,0:T(8,128)(2,1)S(1)}, bf16[1,3,2,128,512]{3,4,2,1,0:T(8,128)(2,1)S(1)}, u32[]{:S(2)}, u32[]{:S(2)}) %collective-permute-start.16) | collective-permute-done | bytes 786464 | tf_op jit(solution)/shard_map/ppermute | solution.py:20
  (121 shorter events, 60.6 us)
Async XLA Ops:
  0.6 11.3 %copy-start.6 = (s32[1,8,1]{1,2,0:T(1,128)S(1)}, s32[1,8,1]{1,2,0:T(1,128)}, u32[]{:S(2)}) copy-start(s32[1,8,1]{1,2,0:T(1,128)} %param.19) | copy-start | bytes 100
  5.1 12.3 %collective-permute-start = (bf16[24,7168]{1,0:T(8,128)(2,1)}, bf16[24,7168]{1,0:T(8,128)(2,1)}, u32[]{:S(2)}, u32[]{:S(2)}) collective-permute-start(bf16[24,7168]{1,0:T(8,128)(2,1)} %get-tuple-element.17), channel_id=1, source_target_pairs={{0,2},{1,3},{2,4},{3,5},{4,6},{5,7},{6,0},{7,1},{8,10},{9,11},{10,... | collective-permute-start | bytes 1032200 | tf_op jit(solution)/shard_map/ppermute | solution.py:81
  7.2 42.4 %collective-permute-start.3 = (bf16[24,7168]{1,0:T(8,128)(2,1)}, bf16[24,7168]{1,0:T(8,128)(2,1)}, u32[]{:S(2)}, u32[]{:S(2)}) collective-permute-start(bf16[24,7168]{1,0:T(8,128)(2,1)} %get-tuple-element.17), channel_id=1, source_target_pairs={{0,1},{1,0},{2,3},{3,2},{4,5},{5,4},{6,7},{7,6},{8,9},{9,8},{10,11... | collective-permute-start | bytes 1032200 | tf_op jit(solution)/shard_map/ppermute | solution.py:75
  17.4 10.4 %collective-permute-start.1 = (bf16[24,7168]{1,0:T(8,128)(2,1)}, bf16[24,7168]{1,0:T(8,128)(2,1)}, u32[]{:S(2)}, u32[]{:S(2)}) collective-permute-start(bf16[24,7168]{1,0:T(8,128)(2,1)} %collective-permute-done), channel_id=1, source_target_pairs={{0,2},{1,3},{2,4},{3,5},{4,6},{5,7},{6,0},{7,1},{8,10},{9,11},{10,... | collective-permute-start | bytes 1032200 | tf_op jit(solution)/shard_map/ppermute | solution.py:81
  17.5 33.9 %collective-permute-start.4 = (bf16[24,7168]{1,0:T(8,128)(2,1)}, bf16[24,7168]{1,0:T(8,128)(2,1)}, u32[]{:S(2)}, u32[]{:S(2)}) collective-permute-start(bf16[24,7168]{1,0:T(8,128)(2,1)} %collective-permute-done), channel_id=1, source_target_pairs={{0,1},{1,0},{2,3},{3,2},{4,5},{5,4},{6,7},{7,6},{8,9},{9,8},{10,11... | collective-permute-start | bytes 1032200 | tf_op jit(solution)/shard_map/ppermute | solution.py:75
  27.8 18.6 %collective-permute-start.2 = (bf16[24,7168]{1,0:T(8,128)(2,1)}, bf16[24,7168]{1,0:T(8,128)(2,1)}, u32[]{:S(2)}, u32[]{:S(2)}) collective-permute-start(bf16[24,7168]{1,0:T(8,128)(2,1)} %collective-permute-done.1), channel_id=1, source_target_pairs={{0,2},{1,3},{2,4},{3,5},{4,6},{5,7},{6,0},{7,1},{8,10},{9,11},{10,... | collective-permute-start | bytes 1032200 | tf_op jit(solution)/shard_map/ppermute | solution.py:81
  27.8 25.3 %collective-permute-start.5 = (bf16[24,7168]{1,0:T(8,128)(2,1)}, bf16[24,7168]{1,0:T(8,128)(2,1)}, u32[]{:S(2)}, u32[]{:S(2)}) collective-permute-start(bf16[24,7168]{1,0:T(8,128)(2,1)} %collective-permute-done.1), channel_id=1, source_target_pairs={{0,1},{1,0},{2,3},{3,2},{4,5},{5,4},{6,7},{7,6},{8,9},{9,8},{10,11... | collective-permute-start | bytes 1032200 | tf_op jit(solution)/shard_map/ppermute | solution.py:75
  41.4 50.5 %all-to-all-start = ((bf16[8,1,2,4,1,128,128]{6,5,3,2,4,1,0:T(8,128)(2,1)}), bf16[8,1,2,4,1,128,128]{6,5,3,2,4,1,0:T(8,128)(2,1)S(1)}, u32[]{:S(2)}, u32[]{:S(2)}) async-start(bf16[8,1,2,4,1,128,128]{6,5,3,2,4,1,0:T(8,128)(2,1)} %bitcast_dynamic-update-slice_fusion), calls=%async_computation | async-start | bytes 4194304 | tf_op jit(solution)/shard_map/all_to_all | solution.py:146
  46.4 26.5 %copy-start.7 = (f32[1536]{0:T(1024)S(1)}, f32[1536]{0:T(1024)}, u32[]{:S(2)}) copy-start(f32[1536]{0:T(1024)} %param.14) | copy-start | bytes 18436
  46.4 25.8 %collective-permute-start.6 = (bf16[24,7168]{1,0:T(8,128)(2,1)}, bf16[24,7168]{1,0:T(8,128)(2,1)S(1)}, u32[]{:S(2)}, u32[]{:S(2)}) collective-permute-start(bf16[24,7168]{1,0:T(8,128)(2,1)} %collective-permute-done.2), channel_id=1, source_target_pairs={{0,1},{1,0},{2,3},{3,2},{4,5},{5,4},{6,7},{7,6},{8,9},{9,8},{10,11... | collective-permute-start | bytes 1032200 | tf_op jit(solution)/shard_map/ppermute | solution.py:75
  94.9 2.7 %slice-start = ((s8[7340032]{0:T(1024)(128)(4,1)}), s8[3145728]{0:T(1024)(128)(4,1)S(1)}, s32[]{:S(2)}) async-start(s8[7340032]{0:T(1024)(128)(4,1)} %bitcast.128), calls=%async_computation.1 | async-start | bytes 6291456
  100.6 9.5 %collective-permute-start.7 = (bf16[24,7168]{1,0:T(8,128)(2,1)S(1)}, bf16[24,7168]{1,0:T(8,128)(2,1)S(1)}, u32[]{:S(2)}, u32[]{:S(2)}) collective-permute-start(bf16[24,7168]{1,0:T(8,128)(2,1)S(1)} %get-tuple-element.28), channel_id=1, source_target_pairs={{0,1},{1,0},{2,3},{3,2},{4,5},{5,4},{6,7},{7,6},{8,9},{9,8},{10,11... | collective-permute-start | bytes 1032200 | tf_op jit(solution)/shard_map/ppermute | solution.py:75
  105.4 6.7 %copy-start = (f32[96,7168]{1,0:T(8,128)}, f32[96,7168]{1,0:T(8,128)S(1)}, u32[]{:S(2)}) copy-start(f32[96,7168]{1,0:T(8,128)S(1)} %fusion.70) | copy-start | bytes 8257540
  110.1 9.0 %collective-permute-start.9 = (bf16[24,7168]{1,0:T(8,128)(2,1)}, bf16[24,7168]{1,0:T(8,128)(2,1)S(1)}, u32[]{:S(2)}, u32[]{:S(2)}) collective-permute-start(bf16[24,7168]{1,0:T(8,128)(2,1)} %get-tuple-element.11), channel_id=1, source_target_pairs={{0,1},{1,0},{2,3},{3,2},{4,5},{5,4},{6,7},{7,6},{8,9},{9,8},{10,11... | collective-permute-start | bytes 1032200 | tf_op jit(solution)/shard_map/ppermute | solution.py:75
  112.9 9.0 %collective-permute-start.8 = (bf16[24,7168]{1,0:T(8,128)(2,1)}, bf16[24,7168]{1,0:T(8,128)(2,1)}, u32[]{:S(2)}, u32[]{:S(2)}) collective-permute-start(bf16[24,7168]{1,0:T(8,128)(2,1)} %fusion.64), channel_id=1, source_target_pairs={{0,2},{1,3},{2,4},{3,5},{4,6},{5,7},{6,0},{7,1},{8,10},{9,11},{10,... | collective-permute-start | bytes 1032200 | tf_op jit(solution)/shard_map/ppermute | solution.py:81
  116.2 12.1 %collective-permute-start.14 = (bf16[1,3,2,128,512]{3,4,2,1,0:T(8,128)(2,1)}, bf16[1,3,2,128,512]{3,4,2,1,0:T(8,128)(2,1)}, u32[]{:S(2)}, u32[]{:S(2)}) collective-permute-start(bf16[1,3,2,128,512]{3,4,2,1,0:T(8,128)(2,1)} %bitcast.136), channel_id=1, source_target_pairs={{0,8},{8,16},{16,24},{24,0},{1,9},{9,17},{17,25},{25,1},{2,10},{10... | collective-permute-start | bytes 2359304 | tf_op jit(solution)/shard_map/ppermute | solution.py:20
  119.0 10.0 %collective-permute-start.11 = (bf16[24,7168]{1,0:T(8,128)(2,1)}, bf16[24,7168]{1,0:T(8,128)(2,1)}, u32[]{:S(2)}, u32[]{:S(2)}) collective-permute-start(bf16[24,7168]{1,0:T(8,128)(2,1)} %get-tuple-element.12), channel_id=1, source_target_pairs={{0,1},{1,0},{2,3},{3,2},{4,5},{5,4},{6,7},{7,6},{8,9},{9,8},{10,11... | collective-permute-start | bytes 1032200 | tf_op jit(solution)/shard_map/ppermute | solution.py:75
  123.9 8.1 %collective-permute-start.10 = (bf16[24,7168]{1,0:T(8,128)(2,1)}, bf16[24,7168]{1,0:T(8,128)(2,1)S(1)}, u32[]{:S(2)}, u32[]{:S(2)}) collective-permute-start(bf16[24,7168]{1,0:T(8,128)(2,1)} %fusion.63), channel_id=1, source_target_pairs={{0,2},{1,3},{2,4},{3,5},{4,6},{5,7},{6,0},{7,1},{8,10},{9,11},{10,... | collective-permute-start | bytes 1032200 | tf_op jit(solution)/shard_map/ppermute | solution.py:81
  128.3 15.8 %collective-permute-start.15 = (bf16[1,3,2,128,512]{3,4,2,1,0:T(8,128)(2,1)}, bf16[1,3,2,128,512]{3,4,2,1,0:T(8,128)(2,1)}, u32[]{:S(2)}, u32[]{:S(2)}) collective-permute-start(bf16[1,3,2,128,512]{3,4,2,1,0:T(8,128)(2,1)} %bitcast.36), channel_id=1, source_target_pairs={{0,16},{8,24},{16,0},{24,8},{1,17},{9,25},{17,1},{25,9},{2,18},{10... | collective-permute-start | bytes 2359304 | tf_op jit(solution)/shard_map/ppermute | solution.py:20
  129.0 19.6 %collective-permute-start.13 = (bf16[24,7168]{1,0:T(8,128)(2,1)}, bf16[24,7168]{1,0:T(8,128)(2,1)}, u32[]{:S(2)}, u32[]{:S(2)}) collective-permute-start(bf16[24,7168]{1,0:T(8,128)(2,1)} %get-tuple-element.13), channel_id=1, source_target_pairs={{0,1},{1,0},{2,3},{3,2},{4,5},{5,4},{6,7},{7,6},{8,9},{9,8},{10,11... | collective-permute-start | bytes 1032200 | tf_op jit(solution)/shard_map/ppermute | solution.py:75
  134.0 14.5 %collective-permute-start.12 = (bf16[24,7168]{1,0:T(8,128)(2,1)}, bf16[24,7168]{1,0:T(8,128)(2,1)}, u32[]{:S(2)}, u32[]{:S(2)}) collective-permute-start(bf16[24,7168]{1,0:T(8,128)(2,1)} %fusion.61), channel_id=1, source_target_pairs={{0,2},{1,3},{2,4},{3,5},{4,6},{5,7},{6,0},{7,1},{8,10},{9,11},{10,... | collective-permute-start | bytes 1032200 | tf_op jit(solution)/shard_map/ppermute | solution.py:81
  140.4 8.2 %copy-start.1 = (bf16[24,7168]{1,0:T(8,128)(2,1)S(1)}, bf16[24,7168]{1,0:T(8,128)(2,1)}, u32[]{:S(2)}) copy-start(bf16[24,7168]{1,0:T(8,128)(2,1)} %param.10) | copy-start | bytes 1032196
  140.4 8.2 %copy-start.5 = (f32[7168]{0:T(1024)S(1)}, f32[7168]{0:T(1024)}, u32[]{:S(2)}) copy-start(f32[7168]{0:T(1024)} %param.16) | copy-start | bytes 86020
  144.1 14.7 %collective-permute-start.16 = (bf16[1,3,2,128,512]{3,4,2,1,0:T(8,128)(2,1)S(1)}, bf16[1,3,2,128,512]{3,4,2,1,0:T(8,128)(2,1)S(1)}, u32[]{:S(2)}, u32[]{:S(2)}) collective-permute-start(bf16[1,3,2,128,512]{3,4,2,1,0:T(8,128)(2,1)S(1)} %bitcast.135), channel_id=1, source_target_pairs={{0,24},{8,0},{16,8},{24,16},{1,25},{9,1},{17,9},{25,17},{2,26},{10... | collective-permute-start | bytes 2359304 | tf_op jit(solution)/shard_map/ppermute | solution.py:20
  (4 other events, 5.6 us)
